TPU v7x, 32 devices: a whole 2x2x4 slice. The times are simulated.
32 devices in a mesh: outer: 4 (over z), dp: 2 (over y), cent: 4 (over x, core).
Axes of the slice: x: 2, y: 2, z: 4, core: 2. Of those that a mesh axis runs over, the one named last changes fastest.
Arguments:
- rows: float32 [2048, 1024], P(('outer', 'dp')), may hold values from -256 to 256
- centroids: float32 [4096, 1024], P(('dp', 'cent')), may hold values from -0.5 to 0.5
Outputs:
- centroid_shift: float32 [4096, 1024], P(('dp', 'cent'))
All inputs are finite; a program needn't handle non-finite values.
Results may differ from a plain program's by a relative error of at most 0.0081.
Values may be sent and summed in bfloat16 or wider, within the bound.
No kernel may reach another device: no remote copies, remote signals or barrier semaphores. Data moves between devices by JAX's collectives and lax.ppermute only.
A program may use at most 64 MiB of HBM per device.

v0:
```python
import jax
import jax.numpy as jnp
from jax import lax
from jax.sharding import PartitionSpec as P


def scores_for(piece, cent_bf, squares):
    product = lax.dot_general(
        piece, cent_bf, (((1,), (1,)), ((), ())), preferred_element_type=jnp.float32
    )
    return 0.5 * (2.0 * product - squares[None, :])


def row_summary(logits):
    local_max = jnp.max(logits, axis=1)
    local_sum = jnp.sum(jnp.exp(logits - local_max[:, None]), axis=1)
    return (local_max, local_sum)


def global_stats(local_max, local_sum):
    row_peak = lax.pmax(local_max, ("dp", "cent"))
    row_mass = lax.psum(local_sum * jnp.exp(local_max - row_peak), ("dp", "cent"))
    return (row_peak, row_mass)


def shards(rows, centroids):
    rows_bf = rows.astype(jnp.bfloat16)
    cent_bf = centroids.astype(jnp.bfloat16)
    squares = jnp.sum(centroids * centroids, axis=1)
    gathered = lax.all_gather(rows_bf, "dp", axis=0, tiled=True)
    logits = scores_for(gathered, cent_bf, squares)
    local_max, local_sum = row_summary(logits)
    row_peak, row_mass = global_stats(local_max, local_sum)
    weights = (jnp.exp(logits - row_peak[:, None]) / row_mass[:, None]).astype(jnp.bfloat16)
    weight_sum = jnp.sum(weights.astype(jnp.float32), axis=0)
    pull = lax.dot_general(
        weights, gathered, (((0,), (0,)), ((), ())), preferred_element_type=jnp.float32
    )
    delta = (pull - weight_sum[:, None] * centroids) / (weight_sum[:, None] + 1.0)
    return lax.psum(delta, "outer") / lax.axis_size("outer")


def solution(mesh):
    return jax.shard_map(
        shards,
        mesh=mesh,
        in_specs=(P(("outer", "dp"), None), P(("dp", "cent"), None)),
        out_specs=P(("dp", "cent"), None),
        check_vma=False,
    )
```

profile of v0, /device:TPU:0, one launch (start us, length us, event | category | flops | bytes accessed | tf_op | source)
XLA Modules:
  0.0 160.0 jit_solution(11891567191275131057)
XLA Ops:
  6.5 0.0 copy-start
  6.5 0.0 all-gather.2.cloned.1.call-start
  6.5 2.2 %convert_element_type.12 = bf16[256,1024]{1,0:T(8,128)(2,1)} convert(f32[256,1024]{1,0:T(8,128)} %param.2) | non-fusion elementwise | flops 262144 | bytes 1572864 | tf_op jit(solution)/shard_map/convert_element_type | solution.py:27
  8.8 0.0 all-gather.2.cloned.1.call-update
  8.8 0.0 all-reduce.2.cloned.1.call-start
  8.9 0.0 copy-done
  8.9 0.2 multiply_reduce_fusion
  9.1 23.9 %all-gather.2.cloned.1.call-done = bf16[512,1024]{1,0:T(8,128)(2,1)} async-done(((bf16[256,1024]{1,0:T(8,128)(2,1)}), bf16[512,1024]{1,0:T(8,128)(2,1)}) %all-gather.2.cloned.1.call-update) | async-done | bytes 1048592 | tf_op jit(solution)/shard_map/all_gather | solution.py:30
  33.0 2.0 %fusion.3 = (f32[512]{0:T(512)S(1)}, f32[512,512]{0,1:T(8,128)S(1)}) fusion(f32[512]{0:T(512)S(1)} %multiply_reduce_fusion, bf16[512,1024]{1,0:T(8,128)(2,1)} %all-gather.2.cloned.1.call-done, f32[512,1024]{1,0:T(8,128)S(1)} %copy-done), kind=kOutput, calls=%fused_computation.12 | convolution fusion | flops 538443264 | bytes 4198400 | tf_op jit(solution)/shard_map/dot_general | solution.py:8
  35.0 12.7 %pmax.7 = f32[512]{0:T(512)S(1)} all-reduce(f32[512]{0:T(512)S(1)} %get-tuple-element.7), channel_id=1, replica_groups=mesh['outer'=4,'dp'=2,'cent'=4] {'dp','cent'}, use_global_device_ids=true, to_apply=%region_2.0 | all-reduce | flops 512 | bytes 4096 | tf_op jit(solution)/shard_map/pmax | solution.py:21
  47.7 0.2 exponential_reduce_fusion
  47.9 11.8 %psum.14 = f32[512]{0:T(512)S(1)} all-reduce(f32[512]{0:T(512)S(1)} %exponential_multiply_fusion), channel_id=1, replica_groups=mesh['outer'=4,'dp'=2,'cent'=4] {'dp','cent'}, use_global_device_ids=true, to_apply=%region_4.0 | all-reduce | flops 512 | bytes 4096 | tf_op jit(solution)/shard_map/psum | solution.py:22
  59.7 0.3 convert_reduce_fusion
  60.0 3.3 %subtract_divide_fusion = f32[512,1024]{1,0:T(8,128)} fusion(f32[512,1024]{1,0:T(8,128)S(1)} %copy-done, bf16[512,512]{0,1:T(8,128)(2,1)S(1)} %get-tuple-element.6, bf16[512,1024]{1,0:T(8,128)(2,1)} %all-gather.2.cloned.1.call-done, f32[512]{0:T(512)S(1)} %broadcast_add_fusion, f32[512]{0:T(512)S(1)} %get-tuple-element.5), kind=kOutput, calls=%fused_computation | convolution fusion | flops 538443776 | bytes 5771264 | tf_op jit(solution)/shard_map/dot_general | solution.py:36
  63.3 0.0 all-reduce.2.cloned.1.call-update
  63.3 86.7 %all-reduce.2.cloned.1.call-done = f32[512,1024]{1,0:T(8,128)} async-done(((f32[512,1024]{1,0:T(8,128)}), f32[512,1024]{1,0:T(8,128)}) %all-reduce.2.cloned.1.call-update) | async-done | bytes 2097168 | tf_op jit(solution)/shard_map/psum | solution.py:40
  150.0 3.2 %broadcast_multiply_fusion = f32[512,1024]{1,0:T(8,128)} fusion(f32[512,1024]{1,0:T(8,128)} %all-reduce.2.cloned.1.call-done), kind=kLoop, calls=%fused_computation.5 | loop fusion | flops 524288 | bytes 4194304 | tf_op jit(solution)/shard_map/div | solution.py:40
  (2 shorter events, 0.0 us)
Async XLA Ops:
  6.5 2.3 %copy-start = (f32[512,1024]{1,0:T(8,128)S(1)}, f32[512,1024]{1,0:T(8,128)}, u32[]{:S(2)}) copy-start(f32[512,1024]{1,0:T(8,128)} %param.3) | copy-start | bytes 6291460
  6.5 26.4 %all-gather.2.cloned.1.call-start = ((), (), s32[]{:S(2)}) async-start(), calls=%async_computation | async-start | bytes 1572864 | tf_op jit(solution)/shard_map/all_gather | solution.py:30
  8.8 141.2 %all-reduce.2.cloned.1.call-start = ((), (), s32[]{:S(2)}) async-start(), calls=%async_computation.1 | async-start | bytes 4194304 | tf_op jit(solution)/shard_map/psum | solution.py:40
Sparse Core Ops, SparseCore 0:
  8.9 23.9 all-gather.1
  63.4 86.5 all-reduce.1
where the time goes:
time: 160 us
  waiting for transfers between devices  111 us (69%)
  blocking collectives  24.5 us (15%)
  between operations  13.4 us (8%)
  other arithmetic  6.15 us (4%)
  matrix products  5.29 us (3%)
    psum x1, waiting for transfers between devices, shards(): return lax.psum(delta, 'outer') / lax.axis_size('outer')  86.7 us
    all_gather x1, waiting for transfers between devices, shards(): gathered = lax.all_gather(rows_bf, 'dp', axis=0, tiled=True)  23.9 us
    pmax x1, blocking collectives, global_stats(): row_peak = lax.pmax(local_max, ('dp', 'cent'))  12.7 us
    psum x1, blocking collectives, global_stats(): lax.psum(local_sum * jnp.exp(local_max - row_peak), ('dp', 'cent'))  11.8 us
    dot_general x1, matrix products, shards(): lax.dot_general(weights, gathered, (((0,), (0,)), ((), ())), preferred_el...  3.3 us
    div x1, other arithmetic, shards(): return lax.psum(delta, 'outer') / lax.axis_size('outer')  3.22 us
  transfers between devices with their start and end apart: 2, of which 2 were waited for; matrix products, arithmetic and copies ran while one was open for 0% of the time, Pallas kernels for 0%

commit v1 on v0

--- a/solution.py
+++ b/solution.py
@@ -2,6 +2,23 @@
 import jax.numpy as jnp
 from jax import lax
 from jax.sharding import PartitionSpec as P
+
+
+def laid_out(blocks, dim):
+    blocks = jnp.moveaxis(blocks, 0, dim)
+    shape = blocks.shape
+    return blocks.reshape(*shape[:dim], shape[dim] * shape[dim + 1], *shape[dim + 2 :])
+
+
+def grow_blocks(x, axis):
+    size, here = (lax.axis_size(axis), lax.axis_index(axis))
+    tiles, apart = (x[None], 1)
+    while apart < size:
+        other = lax.ppermute(tiles, axis, [(i, i ^ apart) for i in range(size)])
+        low = here & apart == 0
+        tiles = jnp.concatenate([jnp.where(low, tiles, other), jnp.where(low, other, tiles)])
+        apart *= 2
+    return tiles
 
 
 def scores_for(piece, cent_bf, squares):
@@ -27,7 +44,7 @@
     rows_bf = rows.astype(jnp.bfloat16)
     cent_bf = centroids.astype(jnp.bfloat16)
     squares = jnp.sum(centroids * centroids, axis=1)
-    gathered = lax.all_gather(rows_bf, "dp", axis=0, tiled=True)
+    gathered = laid_out(grow_blocks(rows_bf, "dp"), 0)
     logits = scores_for(gathered, cent_bf, squares)
     local_max, local_sum = row_summary(logits)
     row_peak, row_mass = global_stats(local_max, local_sum)

time: 160 us -> 151 us (0.944)
  waiting for transfers between devices: 111 us -> 96.5 us
  starting transfers between devices: 0.04 us -> 2.97 us
  other arithmetic: 6.15 us -> 8.91 us
    all_gather x1 -> x0, waiting for transfers between devices: 23.9 us -> none  [shards(): gathered = lax.all_gather(rows_bf, 'dp', axis=0, tiled=True)]
    ppermute x0 -> x1, waiting for transfers between devices: none -> 10.4 us  [grow_blocks(): other = lax.ppermute(tiles, axis, [(i, i ^ apart) for i in range(size)])]
    ppermute x0 -> x1, starting transfers between devices: none -> 2.97 us  [grow_blocks(): other = lax.ppermute(tiles, axis, [(i, i ^ apart) for i in range(size)])]
    convert_element_type x1 -> x0, other arithmetic: 2.24 us -> none  [shards(): rows_bf = rows.astype(jnp.bfloat16)]
    broadcast_in_dim x0 -> x1, other arithmetic: none -> 2.18 us  [grow_blocks(): tiles, apart = (x[None], 1)]
  transfers between devices with their start and end apart: 2 -> 2, of which waited for: 2 -> 2; matrix products, arithmetic and copies ran while one was open for 0% -> 1% of each run, Pallas kernels for 0% -> 0%
where the time goes in v1:
time: 151 us
  waiting for transfers between devices  96.5 us (64%)
  blocking collectives  24.8 us (16%)
  between operations  13.4 us (9%)
  other arithmetic  8.91 us (6%)
  matrix products  4.08 us (3%)
  starting transfers between devices  2.97 us (2%)
    psum x1, waiting for transfers between devices, shards(): return lax.psum(delta, 'outer') / lax.axis_size('outer')  86 us
    pmax x1, blocking collectives, global_stats(): row_peak = lax.pmax(local_max, ('dp', 'cent'))  13 us
    psum x1, blocking collectives, global_stats(): lax.psum(local_sum * jnp.exp(local_max - row_peak), ('dp', 'cent'))  11.8 us
    ppermute x1, waiting for transfers between devices, grow_blocks(): other = lax.ppermute(tiles, axis, [(i, i ^ apart) for i in range(size)])  10.4 us
    dot_general x1, matrix products, shards(): lax.dot_general(weights, gathered, (((0,), (0,)), ((), ())), preferred_el...  3.3 us
    div x1, other arithmetic, shards(): return lax.psum(delta, 'outer') / lax.axis_size('outer')  3.22 us
  transfers between devices with their start and end apart: 2, of which 2 were waited for; matrix products, arithmetic and copies ran while one was open for 1% of the time, Pallas kernels for 0%

profile of v1, /device:TPU:0, one launch (start us, length us, event | category | flops | bytes accessed | tf_op | source)
XLA Modules:
  0.0 150.9 jit_solution(1358231808904108760)
XLA Ops:
  6.5 0.0 copy-start.2
  6.5 0.0 all-reduce.2.cloned.1.call-start
  6.5 2.2 %convert_bitcast_fusion = bf16[1,256,1024]{2,1,0:T(8,128)(2,1)} fusion(f32[256,1024]{1,0:T(8,128)} %param.2), kind=kLoop, calls=%fused_computation.11 | loop fusion | flops 262144 | bytes 1572864 | tf_op jit(solution)/shard_map/broadcast_in_dim | solution.py:15
  8.7 3.0 %collective-permute-start = (bf16[1,256,1024]{2,1,0:T(8,128)(2,1)}, bf16[1,256,1024]{2,1,0:T(8,128)(2,1)}, u32[]{:S(2)}, u32[]{:S(2)}) collective-permute-start(bf16[1,256,1024]{2,1,0:T(8,128)(2,1)} %convert_bitcast_fusion), channel_id=1, source_target_pairs={{0,4},{4,0},{1,5},{5,1},{2,6},{6,2},{3,7},{7,3},{8,12},{12,8},{9,1... | collective-permute-start | bytes 1572872 | tf_op jit(solution)/shard_map/ppermute | solution.py:17
  11.7 1.8 %multiply_reduce_fusion = f32[512]{0:T(512)S(1)} fusion(f32[512,1024]{1,0:T(8,128)} %param.3), kind=kLoop, calls=%fused_computation.1 | loop fusion | flops 1048064 | bytes 2099200 | tf_op jit(solution)/shard_map/reduce_sum | solution.py:46
  13.5 0.0 copy-start
  13.5 10.4 %collective-permute-done = bf16[1,256,1024]{2,1,0:T(8,128)(2,1)} collective-permute-done((bf16[1,256,1024]{2,1,0:T(8,128)(2,1)}, bf16[1,256,1024]{2,1,0:T(8,128)(2,1)}, u32[]{:S(2)}, u32[]{:S(2)}) %collective-permute-start) | collective-permute-done | bytes 524320 | tf_op jit(solution)/shard_map/ppermute | solution.py:17
  23.9 0.0 copy-done.2
  23.9 1.1 broadcast_select_fusion.1
  25.1 0.1 pad_maximum_fusion
  25.2 0.0 copy-start.1
  25.2 0.0 copy-done
  25.2 0.8 fusion.3
  26.0 0.2 copy-done.1
  26.2 13.0 %pmax.7 = f32[512]{0:T(512)S(1)} all-reduce(f32[512]{0:T(512)S(1)} %get-tuple-element.9), channel_id=1, replica_groups=mesh['outer'=4,'dp'=2,'cent'=4] {'dp','cent'}, use_global_device_ids=true, to_apply=%region_2.3 | all-reduce | flops 512 | bytes 4096 | tf_op jit(solution)/shard_map/pmax | solution.py:38
  39.2 0.2 exponential_reduce_fusion
  39.4 11.8 %psum.14 = f32[512]{0:T(512)S(1)} all-reduce(f32[512]{0:T(512)S(1)} %exponential_multiply_fusion), channel_id=1, replica_groups=mesh['outer'=4,'dp'=2,'cent'=4] {'dp','cent'}, use_global_device_ids=true, to_apply=%region_4.5 | all-reduce | flops 512 | bytes 4096 | tf_op jit(solution)/shard_map/psum | solution.py:39
  51.2 0.3 convert_reduce_fusion
  51.4 3.3 %subtract_divide_fusion = f32[512,1024]{1,0:T(8,128)} fusion(f32[512,1024]{1,0:T(8,128)S(1)} %copy-done, bf16[512,512]{0,1:T(8,128)(2,1)S(1)} %get-tuple-element.6, bf16[512,1024]{1,0:T(8,128)(2,1)} %bitcast.9, f32[512]{0:T(512)S(1)} %broadcast_add_fusion, f32[512]{0:T(512)S(1)} %get-tuple-element.5), kind=kOutput, calls=%fused_computation | convolution fusion | flops 538443776 | bytes 5771264 | tf_op jit(solution)/shard_map/dot_general | solution.py:53
  54.7 0.0 all-reduce.2.cloned.1.call-update
  54.8 86.0 %all-reduce.2.cloned.1.call-done = f32[512,1024]{1,0:T(8,128)} async-done(((f32[512,1024]{1,0:T(8,128)}), f32[512,1024]{1,0:T(8,128)}) %all-reduce.2.cloned.1.call-update) | async-done | bytes 2097168 | tf_op jit(solution)/shard_map/psum | solution.py:57
  140.8 3.2 %broadcast_multiply_fusion = f32[512,1024]{1,0:T(8,128)} fusion(f32[512,1024]{1,0:T(8,128)} %all-reduce.2.cloned.1.call-done), kind=kLoop, calls=%fused_computation.6 | loop fusion | flops 524288 | bytes 4194304 | tf_op jit(solution)/shard_map/div | solution.py:57
  (2 shorter events, 0.0 us)
Async XLA Ops:
  6.5 17.4 %copy-start.2 = (f32[256,1024]{1,0:T(8,128)S(1)}, f32[256,1024]{1,0:T(8,128)}, u32[]{:S(2)}) copy-start(f32[256,1024]{1,0:T(8,128)} %param.2) | copy-start | bytes 3145732
  6.5 134.3 %all-reduce.2.cloned.1.call-start = ((), (), s32[]{:S(2)}) async-start(), calls=%async_computation | async-start | bytes 4194304 | tf_op jit(solution)/shard_map/psum | solution.py:57
  8.7 15.2 %collective-permute-start = (bf16[1,256,1024]{2,1,0:T(8,128)(2,1)}, bf16[1,256,1024]{2,1,0:T(8,128)(2,1)}, u32[]{:S(2)}, u32[]{:S(2)}) collective-permute-start(bf16[1,256,1024]{2,1,0:T(8,128)(2,1)} %convert_bitcast_fusion), channel_id=1, source_target_pairs={{0,4},{4,0},{1,5},{5,1},{2,6},{6,2},{3,7},{7,3},{8,12},{12,8},{9,1... | collective-permute-start | bytes 1572872 | tf_op jit(solution)/shard_map/ppermute | solution.py:17
  13.5 11.7 %copy-start = (f32[512,1024]{1,0:T(8,128)S(1)}, f32[512,1024]{1,0:T(8,128)}, u32[]{:S(2)}) copy-start(f32[512,1024]{1,0:T(8,128)} %param.3) | copy-start | bytes 6291460
  25.2 1.0 copy-start.1
Sparse Core Ops, SparseCore 0:
  54.9 85.8 all-reduce.1
